TPU v7x, 512 devices: a whole 4x4x16 slice. The times are simulated.
512 devices in a mesh: chan: 32 (over x_lo, z), freq: 16 (over y, x_hi, core).
Axes of the slice: x: 4 (x_hi: 2, x_lo: 2; x = x_hi * 2 + x_lo), y: 4, z: 16, core: 2. Of those that a mesh axis runs over, the one named last changes fastest.
Arguments:
- traces: bfloat16 [4096, 81920], P('chan', 'freq'), may hold values from -2000 to 2000
- kept_bins: int32 [128], replicated, may hold values from 1 to 255, as said below
- round_masks: int32 [2], replicated, may hold values from 1 to 31, as said below
Outputs:
- cross_spectra: float32 [2, 128, 2, 4096, 128], P(None, 'freq', None, 'chan')
- auto_spectra: float32 [128, 2, 4096, 128], P('freq', None, 'chan')
Inputs may be any that keep to these rules, and one draw needn't show every extreme that they name: `kept_bins`: 128 distinct bin numbers in increasing order; 1 and 255 are among them. `round_masks`: 2 distinct numbers; in round r channel block b is paired with block b XOR round_masks[r].
All inputs are finite; a program needn't handle non-finite values.
Results may differ from a plain program's by a relative error of at most 0.0066.
Values may be sent and summed in bfloat16 or wider, within the bound.
No kernel may reach another device: no remote copies, remote signals or barrier semaphores. Data moves between devices by JAX's collectives and lax.ppermute only.
A program may use at most 64 MiB of HBM per device.

v0:
```python
import math

import jax
import jax.numpy as jnp
from jax import lax
from jax.sharding import PartitionSpec as P

NS = 512
ROUNDS = 2


EPSILON = 1e-06


def shifted(block, axis, distance):
    devices = range(lax.axis_size(axis))
    route = [(i - distance, i) for i in devices if i - distance in devices]
    return lax.ppermute(block, axis, route)


def swapped(shard, axis, distance):
    return lax.ppermute(shard, axis, [(i, i ^ 1 << distance) for i in range(lax.axis_size(axis))])


def dft_table(kept_bins):
    sample_index = jnp.arange(NS, dtype=jnp.int32)
    phase_index = kept_bins[:, None] * sample_index[None, :] % NS
    angles = phase_index.astype(jnp.float32) * jnp.float32(2.0 * math.pi / NS)
    hann_taper = 0.5 - 0.5 * jnp.cos(
        sample_index.astype(jnp.float32) * jnp.float32(2.0 * math.pi / NS)
    )
    stacked = jnp.stack([hann_taper * jnp.cos(angles), -hann_taper * jnp.sin(angles)], axis=1)
    return stacked.reshape(kept_bins.shape[0] * 2, NS).astype(jnp.bfloat16)


def correlate(left_block, right_block, windows):
    products = jnp.einsum(
        "kpwc,kqwd->kpqcd", left_block, right_block, preferred_element_type=jnp.float32
    )
    real_part = products[:, 0, 0] + products[:, 1, 1]
    imag_part = products[:, 1, 0] - products[:, 0, 1]
    return jnp.stack([real_part, imag_part], axis=1) * (1.0 / math.sqrt(windows))


def body(traces, kept_bins, round_masks):
    channels, samples_here = traces.shape
    hop_length = NS // 2
    frames = samples_here // hop_length
    keep_count = kept_bins.shape[0]
    transform = dft_table(kept_bins)
    following = shifted(traces[:, :hop_length], "freq", -1)
    extended = jnp.concatenate([traces, following], axis=1).reshape(
        channels, frames + 1, hop_length
    )
    spectra = jnp.einsum(
        "kn,cjn->kjc",
        transform[:, :hop_length],
        extended[:, :-1],
        preferred_element_type=jnp.float32,
    )
    spectra = spectra + jnp.einsum(
        "kn,cjn->kjc",
        transform[:, hop_length:],
        extended[:, 1:],
        preferred_element_type=jnp.float32,
    )
    rounded = spectra.astype(jnp.bfloat16).reshape(keep_count, 2, frames * channels)
    windows = frames * lax.axis_size("freq")
    values = rounded.astype(jnp.float32).reshape(keep_count, 2, frames, channels)
    partial_power = jnp.sum(values * values, axis=(1, 2))
    power_mean = lax.psum(partial_power, "freq") / windows
    whitened = (values * lax.rsqrt(power_mean + EPSILON)[:, None, None, :]).astype(jnp.bfloat16)
    arrived_bins = lax.all_to_all(
        whitened.reshape(keep_count, 2, frames * channels),
        "freq",
        split_axis=0,
        concat_axis=2,
        tiled=True,
    )
    own_block = arrived_bins.reshape(-1, 2, windows, channels)
    auto_spectra = correlate(own_block, own_block, windows)
    blocks_count = lax.axis_size("chan")
    crosses = []
    levels = blocks_count.bit_length() - 1
    for round_no in range(ROUNDS):
        round_mask = round_masks[round_no]
        carried = own_block
        for which_bit in range(levels):
            arrived = swapped(carried, "chan", which_bit)
            chosen = jnp.bitwise_and(jnp.right_shift(round_mask, which_bit), 1) == 1
            carried = jnp.where(chosen, arrived, carried)
        crosses.append(correlate(own_block, carried, windows))
    return (jnp.stack(crosses), auto_spectra)


def solution(mesh):
    placed = (P("chan", "freq"), P(), P())
    return jax.shard_map(
        body,
        mesh=mesh,
        in_specs=placed,
        out_specs=(P(None, "freq", None, "chan", None), P("freq", None, "chan", None)),
        check_vma=False,
    )
```

profile of v0, /device:TPU:1, one launch (start us, length us, event | category | flops | bytes accessed | tf_op | source)
XLA Modules:
  0.0 897.1 jit_solution(6204677982949660020)
XLA Ops:
  7.2 1.8 copy.73
  9.0 8.7 collective-permute-start
  17.8 1.3 multiply_convert_fusion.2
  19.1 0.3 copy.75
  19.6 0.6 fusion.23
  20.2 0.7 fusion
  20.9 0.8 reduce_sum.21
  21.7 1.8 convert_bitcast_fusion
  23.6 2.4 copy.77
  26.0 2.5 reshape.423
  28.5 138.5 %all-reduce.2.cloned.1.call-done = f32[128,128]{1,0:T(8,128)} async-done(((f32[128,128]{1,0:T(8,128)}), f32[128,128]{1,0:T(8,128)}) %all-reduce.2.cloned.1.call-update) | async-done | bytes 65552 | tf_op jit(solution)/shard_map/psum | solution.py:71
  166.9 0.9 add_rsqrt_fusion
  167.9 1.2 mul.152
  169.1 2.9 copy.80
  172.0 2.7 multiply_convert_fusion
  174.7 25.7 %all_to_all.15 = bf16[128,2,2560]{2,1,0:T(2,128)(2,1)S(1)} all-to-all(bf16[128,2,2560]{2,1,0:T(2,128)(2,1)S(1)} %multiply_convert_fusion), channel_id=1, replica_groups=mesh['chan'=32,'freq'=16] {'freq'}, dimensions={0} | all-to-all | bytes 2621440 | tf_op jit(solution)/shard_map/all_to_all | solution.py:73
  200.4 0.7 copy.106
  201.1 1.6 reshape.422
  202.8 2.9 collective-permute-start.1
  205.7 0.6 fusion.25
  207.6 26.4 %collective-permute-done.1 = bf16[8,2,320,128]{3,2,1,0:T(8,128)(2,1)S(1)} collective-permute-done((bf16[8,2,320,128]{3,2,1,0:T(8,128)(2,1)S(1)}, bf16[8,2,320,128]{3,2,1,0:T(8,128)(2,1)S(1)}, u32[]{:S(2)}, u32[]{:S(2)}) %collective-permute-start.1) | collective-permute-done | bytes 1310752 | tf_op jit(solution)/shard_map/ppermute | solution.py:22
  234.0 0.2 broadcast_select_fusion.4
  234.2 4.0 collective-permute-start.2
  238.2 2.2 collective-permute-start.6
  241.0 82.0 %collective-permute-done.2 = bf16[8,2,320,128]{3,2,1,0:T(8,128)(2,1)S(1)} collective-permute-done((bf16[8,2,320,128]{3,2,1,0:T(8,128)(2,1)S(1)}, bf16[8,2,320,128]{3,2,1,0:T(8,128)(2,1)S(1)}, u32[]{:S(2)}, u32[]{:S(2)}) %collective-permute-start.2) | collective-permute-done | bytes 1310752 | tf_op jit(solution)/shard_map/ppermute | solution.py:22
  323.1 0.1 broadcast_select_fusion.5
  323.2 6.9 collective-permute-start.3
  330.8 24.1 %collective-permute-done.6 = bf16[8,2,320,128]{3,2,1,0:T(8,128)(2,1)S(1)} collective-permute-done((bf16[8,2,320,128]{3,2,1,0:T(8,128)(2,1)S(1)}, bf16[8,2,320,128]{3,2,1,0:T(8,128)(2,1)S(1)}, u32[]{:S(2)}, u32[]{:S(2)}) %collective-permute-start.6) | collective-permute-done | bytes 1310752 | tf_op jit(solution)/shard_map/ppermute | solution.py:22
  354.9 0.1 broadcast_select_fusion.1
  355.0 31.4 %collective-permute-start.7 = (bf16[8,2,320,128]{3,2,1,0:T(8,128)(2,1)S(1)}, bf16[8,2,320,128]{3,2,1,0:T(8,128)(2,1)S(1)}, u32[]{:S(2)}, u32[]{:S(2)}) collective-permute-start(bf16[8,2,320,128]{3,2,1,0:T(8,128)(2,1)S(1)} %broadcast_select_fusion.1), channel_id=1, source_target_pairs={{0,64},{16,80},{32,96},{48,112},{64,0},{80,16},{96,32},{112,48},{1... | collective-permute-start | bytes 3932168 | tf_op jit(solution)/shard_map/ppermute | solution.py:22
  387.0 223.5 %collective-permute-done.3 = bf16[8,2,320,128]{3,2,1,0:T(8,128)(2,1)S(1)} collective-permute-done((bf16[8,2,320,128]{3,2,1,0:T(8,128)(2,1)S(1)}, bf16[8,2,320,128]{3,2,1,0:T(8,128)(2,1)S(1)}, u32[]{:S(2)}, u32[]{:S(2)}) %collective-permute-start.3) | collective-permute-done | bytes 1310752 | tf_op jit(solution)/shard_map/ppermute | solution.py:22
  610.7 15.1 %collective-permute-start.4 = (bf16[8,2,320,128]{3,2,1,0:T(8,128)(2,1)S(1)}, bf16[8,2,320,128]{3,2,1,0:T(8,128)(2,1)S(1)}, u32[]{:S(2)}, u32[]{:S(2)}) collective-permute-start(bf16[8,2,320,128]{3,2,1,0:T(8,128)(2,1)S(1)} %broadcast_select_fusion.6), channel_id=1, source_target_pairs={{0,128},{16,144},{32,160},{48,176},{64,192},{80,208},{96,224},{112... | collective-permute-start | bytes 3932168 | tf_op jit(solution)/shard_map/ppermute | solution.py:22
  626.4 41.1 %collective-permute-done.7 = bf16[8,2,320,128]{3,2,1,0:T(8,128)(2,1)S(1)} collective-permute-done((bf16[8,2,320,128]{3,2,1,0:T(8,128)(2,1)S(1)}, bf16[8,2,320,128]{3,2,1,0:T(8,128)(2,1)S(1)}, u32[]{:S(2)}, u32[]{:S(2)}) %collective-permute-start.7) | collective-permute-done | bytes 1310752 | tf_op jit(solution)/shard_map/ppermute | solution.py:22
  667.5 1.2 broadcast_select_fusion.2
  668.7 126.2 %collective-permute-start.8 = (bf16[8,2,320,128]{3,2,1,0:T(8,128)(2,1)}, bf16[8,2,320,128]{3,2,1,0:T(8,128)(2,1)}, u32[]{:S(2)}, u32[]{:S(2)}) collective-permute-start(bf16[8,2,320,128]{3,2,1,0:T(8,128)(2,1)} %broadcast_select_fusion.2), channel_id=1, source_target_pairs={{0,128},{16,144},{32,160},{48,176},{64,192},{80,208},{96,224},{112... | collective-permute-start | bytes 3932168 | tf_op jit(solution)/shard_map/ppermute | solution.py:22
  795.5 1.2 broadcast_select_fusion.7
  796.7 2.5 collective-permute-start.5
  801.1 1.6 reshape.427
  802.8 0.8 convolution_bitcast_fusion
  803.6 48.3 %collective-permute-done.8 = bf16[8,2,320,128]{3,2,1,0:T(8,128)(2,1)} collective-permute-done((bf16[8,2,320,128]{3,2,1,0:T(8,128)(2,1)}, bf16[8,2,320,128]{3,2,1,0:T(8,128)(2,1)}, u32[]{:S(2)}, u32[]{:S(2)}) %collective-permute-start.8) | collective-permute-done | bytes 1310752 | tf_op jit(solution)/shard_map/ppermute | solution.py:22
  851.9 2.5 broadcast_select_fusion.3
  854.4 2.3 collective-permute-start.9
  856.9 1.3 copy.88
  858.3 2.1 convolution_bitcast_fusion.2
  860.5 25.1 %collective-permute-done.9 = bf16[8,2,320,128]{3,2,1,0:T(8,128)(2,1)} collective-permute-done((bf16[8,2,320,128]{3,2,1,0:T(8,128)(2,1)}, bf16[8,2,320,128]{3,2,1,0:T(8,128)(2,1)}, u32[]{:S(2)}, u32[]{:S(2)}) %collective-permute-start.9) | collective-permute-done | bytes 1310752 | tf_op jit(solution)/shard_map/ppermute | solution.py:22
  885.7 2.1 convolution_bitcast_fusion.1
  888.2 0.2 pad_maximum_fusion
  888.4 1.8 copy.87
  (27 shorter events, 1.3 us)
Async XLA Ops:
  7.2 10.6 %copy-start.2 = (s32[128]{0:T(128)S(1)}, s32[128]{0:T(128)}, u32[]{:S(2)}) copy-start(s32[128]{0:T(128)} %param.4) | copy-start | bytes 1540
  7.2 159.8 %all-reduce.2.cloned.1.call-start = ((), (), s32[]{:S(2)}) async-start(), calls=%async_computation.1 | async-start | bytes 131072 | tf_op jit(solution)/shard_map/psum | solution.py:71
  9.0 10.5 %collective-permute-start = (bf16[128,256]{0,1:T(8,128)(2,1)S(1)}, bf16[128,256]{0,1:T(8,128)(2,1)S(1)}, u32[]{:S(2)}, u32[]{:S(2)}) collective-permute-start(bf16[128,256]{0,1:T(8,128)(2,1)S(1)} %slice.76), channel_id=1, source_target_pairs={{1,0},{2,1},{3,2},{4,3},{5,4},{6,5},{7,6},{8,7},{9,8},{10,9},{11,1... | collective-permute-start | bytes 196616 | tf_op jit(solution)/shard_map/ppermute | solution.py:18
  169.1 2.9 copy-start
  201.1 4.6 copy-start.1
  202.8 31.3 %collective-permute-start.1 = (bf16[8,2,320,128]{3,2,1,0:T(8,128)(2,1)S(1)}, bf16[8,2,320,128]{3,2,1,0:T(8,128)(2,1)S(1)}, u32[]{:S(2)}, u32[]{:S(2)}) collective-permute-start(bf16[8,2,320,128]{3,2,1,0:T(8,128)(2,1)S(1)} %reshape.422), channel_id=1, source_target_pairs={{0,16},{16,0},{32,48},{48,32},{64,80},{80,64},{96,112},{112,96},{1... | collective-permute-start | bytes 3932168 | tf_op jit(solution)/shard_map/ppermute | solution.py:22
  234.2 88.9 %collective-permute-start.2 = (bf16[8,2,320,128]{3,2,1,0:T(8,128)(2,1)S(1)}, bf16[8,2,320,128]{3,2,1,0:T(8,128)(2,1)S(1)}, u32[]{:S(2)}, u32[]{:S(2)}) collective-permute-start(bf16[8,2,320,128]{3,2,1,0:T(8,128)(2,1)S(1)} %get-tuple-element.14), channel_id=1, source_target_pairs={{0,32},{16,48},{32,0},{48,16},{64,96},{80,112},{96,64},{112,80},{1... | collective-permute-start | bytes 3932168 | tf_op jit(solution)/shard_map/ppermute | solution.py:22
  238.2 116.7 %collective-permute-start.6 = (bf16[8,2,320,128]{3,2,1,0:T(8,128)(2,1)S(1)}, bf16[8,2,320,128]{3,2,1,0:T(8,128)(2,1)S(1)}, u32[]{:S(2)}, u32[]{:S(2)}) collective-permute-start(bf16[8,2,320,128]{3,2,1,0:T(8,128)(2,1)S(1)} %get-tuple-element.15), channel_id=1, source_target_pairs={{0,32},{16,48},{32,0},{48,16},{64,96},{80,112},{96,64},{112,80},{1... | collective-permute-start | bytes 3932168 | tf_op jit(solution)/shard_map/ppermute | solution.py:22
  323.2 287.3 %collective-permute-start.3 = (bf16[8,2,320,128]{3,2,1,0:T(8,128)(2,1)S(1)}, bf16[8,2,320,128]{3,2,1,0:T(8,128)(2,1)S(1)}, u32[]{:S(2)}, u32[]{:S(2)}) collective-permute-start(bf16[8,2,320,128]{3,2,1,0:T(8,128)(2,1)S(1)} %broadcast_select_fusion.5), channel_id=1, source_target_pairs={{0,64},{16,80},{32,96},{48,112},{64,0},{80,16},{96,32},{112,48},{1... | collective-permute-start | bytes 3932168 | tf_op jit(solution)/shard_map/ppermute | solution.py:22
  355.0 312.5 %collective-permute-start.7 = (bf16[8,2,320,128]{3,2,1,0:T(8,128)(2,1)S(1)}, bf16[8,2,320,128]{3,2,1,0:T(8,128)(2,1)S(1)}, u32[]{:S(2)}, u32[]{:S(2)}) collective-permute-start(bf16[8,2,320,128]{3,2,1,0:T(8,128)(2,1)S(1)} %broadcast_select_fusion.1), channel_id=1, source_target_pairs={{0,64},{16,80},{32,96},{48,112},{64,0},{80,16},{96,32},{112,48},{1... | collective-permute-start | bytes 3932168 | tf_op jit(solution)/shard_map/ppermute | solution.py:22
  610.7 184.8 %collective-permute-start.4 = (bf16[8,2,320,128]{3,2,1,0:T(8,128)(2,1)S(1)}, bf16[8,2,320,128]{3,2,1,0:T(8,128)(2,1)S(1)}, u32[]{:S(2)}, u32[]{:S(2)}) collective-permute-start(bf16[8,2,320,128]{3,2,1,0:T(8,128)(2,1)S(1)} %broadcast_select_fusion.6), channel_id=1, source_target_pairs={{0,128},{16,144},{32,160},{48,176},{64,192},{80,208},{96,224},{112... | collective-permute-start | bytes 3932168 | tf_op jit(solution)/shard_map/ppermute | solution.py:22
  668.7 183.2 %collective-permute-start.8 = (bf16[8,2,320,128]{3,2,1,0:T(8,128)(2,1)}, bf16[8,2,320,128]{3,2,1,0:T(8,128)(2,1)}, u32[]{:S(2)}, u32[]{:S(2)}) collective-permute-start(bf16[8,2,320,128]{3,2,1,0:T(8,128)(2,1)} %broadcast_select_fusion.2), channel_id=1, source_target_pairs={{0,128},{16,144},{32,160},{48,176},{64,192},{80,208},{96,224},{112... | collective-permute-start | bytes 3932168 | tf_op jit(solution)/shard_map/ppermute | solution.py:22
  796.7 61.5 %collective-permute-start.5 = (bf16[8,2,320,128]{3,2,1,0:T(8,128)(2,1)}, bf16[8,2,320,128]{3,2,1,0:T(8,128)(2,1)}, u32[]{:S(2)}, u32[]{:S(2)}) collective-permute-start(bf16[8,2,320,128]{3,2,1,0:T(8,128)(2,1)} %broadcast_select_fusion.7), channel_id=1, source_target_pairs={{0,256},{16,272},{32,288},{48,304},{64,320},{80,336},{96,352},{112... | collective-permute-start | bytes 3932168 | tf_op jit(solution)/shard_map/ppermute | solution.py:22
  854.4 31.3 %collective-permute-start.9 = (bf16[8,2,320,128]{3,2,1,0:T(8,128)(2,1)}, bf16[8,2,320,128]{3,2,1,0:T(8,128)(2,1)}, u32[]{:S(2)}, u32[]{:S(2)}) collective-permute-start(bf16[8,2,320,128]{3,2,1,0:T(8,128)(2,1)} %broadcast_select_fusion.3), channel_id=1, source_target_pairs={{0,256},{16,272},{32,288},{48,304},{64,320},{80,336},{96,352},{112... | collective-permute-start | bytes 3932168 | tf_op jit(solution)/shard_map/ppermute | solution.py:22
Sparse Core Ops, SparseCore 0:
  21.9 145.0 all-reduce.1
where the time goes:
time: 899 us; the launch traced here: 897 us
  waiting for transfers between devices  609 us (68%)
  starting transfers between devices  202 us (22%)
  blocking collectives  25.7 us (3%)
  between operations  20.8 us (2%)
  local copies, waits for them, and re-layouts  19.1 us (2%)
  other arithmetic  13.9 us (2%)
    ppermute x9, waiting for transfers between devices, swapped(): lax.ppermute(shard, axis, [(i, i ^ 1 << distance) for i in range(lax.axis...  471 us
    ppermute x9, starting transfers between devices, swapped(): lax.ppermute(shard, axis, [(i, i ^ 1 << distance) for i in range(lax.axis...  193 us
    psum x1, waiting for transfers between devices, body(): power_mean = lax.psum(partial_power, 'freq') / windows  138 us
    all_to_all x1, blocking collectives, body(): lax.all_to_all(whitened.reshape(keep_count, 2, frames * channels), 'freq'...  25.7 us
  transfers between devices with their start and end apart: 11, of which 8 were waited for; matrix products, arithmetic and copies ran while one was open for 2% of the time, Pallas kernels for 0%

commit v1 on v0

--- a/solution.py
+++ b/solution.py
@@ -1,3 +1,4 @@
+import functools
 import math
 
 import jax
@@ -18,8 +19,8 @@
     return lax.ppermute(block, axis, route)
 
 
-def swapped(shard, axis, distance):
-    return lax.ppermute(shard, axis, [(i, i ^ 1 << distance) for i in range(lax.axis_size(axis))])
+def xor_moved(block, axis, mask):
+    return lax.ppermute(block, axis, [(i, i ^ mask) for i in range(lax.axis_size(axis))])
 
 
 def dft_table(kept_bins):
@@ -66,30 +67,20 @@
     )
     rounded = spectra.astype(jnp.bfloat16).reshape(keep_count, 2, frames * channels)
     windows = frames * lax.axis_size("freq")
-    values = rounded.astype(jnp.float32).reshape(keep_count, 2, frames, channels)
-    partial_power = jnp.sum(values * values, axis=(1, 2))
-    power_mean = lax.psum(partial_power, "freq") / windows
-    whitened = (values * lax.rsqrt(power_mean + EPSILON)[:, None, None, :]).astype(jnp.bfloat16)
-    arrived_bins = lax.all_to_all(
-        whitened.reshape(keep_count, 2, frames * channels),
-        "freq",
-        split_axis=0,
-        concat_axis=2,
-        tiled=True,
-    )
-    own_block = arrived_bins.reshape(-1, 2, windows, channels)
+    arrived_bins = lax.all_to_all(rounded, "freq", split_axis=0, concat_axis=2, tiled=True)
+    values = arrived_bins.astype(jnp.float32).reshape(-1, 2, windows, channels)
+    power_mean = jnp.sum(values * values, axis=(1, 2)) / windows
+    own_block = (values * lax.rsqrt(power_mean + EPSILON)[:, None, None, :]).astype(jnp.bfloat16)
     auto_spectra = correlate(own_block, own_block, windows)
     blocks_count = lax.axis_size("chan")
+    branches = [
+        functools.partial(xor_moved, axis="chan", mask=mask) for mask in range(1, blocks_count)
+    ]
     crosses = []
-    levels = blocks_count.bit_length() - 1
     for round_no in range(ROUNDS):
-        round_mask = round_masks[round_no]
-        carried = own_block
-        for which_bit in range(levels):
-            arrived = swapped(carried, "chan", which_bit)
-            chosen = jnp.bitwise_and(jnp.right_shift(round_mask, which_bit), 1) == 1
-            carried = jnp.where(chosen, arrived, carried)
-        crosses.append(correlate(own_block, carried, windows))
+        which = jnp.clip(round_masks[round_no] - 1, 0, blocks_count - 2)
+        partner = lax.switch(which, branches, own_block)
+        crosses.append(correlate(own_block, partner, windows))
     return (jnp.stack(crosses), auto_spectra)
 
 

time: 899 us -> 236 us (0.26)
  waiting for transfers between devices: 609 us -> 162 us
  starting transfers between devices: 202 us -> 32.5 us
  blocking collectives: 25.7 us -> 0 us
  between operations: 20.8 us -> 2.17 us
    ppermute x9 -> x2, waiting for transfers between devices: 471 us -> 144 us  [xor_moved(): lax.ppermute(block, axis, [(i, i ^ mask) for i in range(lax.axis_size(axi...]
    ppermute x9 -> x2, starting transfers between devices: 193 us -> 18.3 us  [xor_moved(): lax.ppermute(block, axis, [(i, i ^ mask) for i in range(lax.axis_size(axi...]
    psum x1 -> x0, waiting for transfers between devices: 138 us -> none  [body(): power_mean = lax.psum(partial_power, 'freq') / windows]
    all_to_all x1 -> x0, blocking collectives: 25.7 us -> none  [body(): lax.all_to_all(whitened.reshape(keep_count, 2, frames * channels), 'freq'...]
    all_to_all x0 -> x1, waiting for transfers between devices: none -> 18 us  [body(): lax.all_to_all(rounded, 'freq', split_axis=0, concat_axis=2, tiled=True)]
  transfers between devices with their start and end apart: 11 -> 4, of which waited for: 8 -> 3; matrix products, arithmetic and copies ran while one was open for 2% -> 1% of each run, Pallas kernels for 0% -> 0%
where the time goes in v1:
time: 236 us; the launch traced here: 235 us
  waiting for transfers between devices  162 us (69%)
  starting transfers between devices  32.5 us (14%)
  local copies, waits for them, and re-layouts  20 us (8%)
  other arithmetic  10.6 us (4%)
  matrix products  7.61 us (3%)
    ppermute x2, waiting for transfers between devices, xor_moved(): lax.ppermute(block, axis, [(i, i ^ mask) for i in range(lax.axis_size(axi...  144 us
    ppermute x2, starting transfers between devices, xor_moved(): lax.ppermute(block, axis, [(i, i ^ mask) for i in range(lax.axis_size(axi...  18.3 us
    all_to_all x1, waiting for transfers between devices, body(): lax.all_to_all(rounded, 'freq', split_axis=0, concat_axis=2, tiled=True)  18 us
    ppermute x1, starting transfers between devices, shifted(): return lax.ppermute(block, axis, route)  8.75 us
    unnamed x19, local copies, waits for them, and re-layouts  7.05 us
    all_to_all x1, starting transfers between devices, body(): lax.all_to_all(rounded, 'freq', split_axis=0, concat_axis=2, tiled=True)  5.47 us
    convert_element_type x2, local copies, waits for them, and re-layouts, body(): values = arrived_bins.astype(jnp.float32).reshape(-1, 2, windows, channels)  5.44 us
    dot_general x3, matrix products, correlate(): jnp.einsum('kpwc,kqwd->kpqcd', left_block, right_block, preferred_element...  5.42 us
  transfers between devices with their start and end apart: 4, of which 3 were waited for; matrix products, arithmetic and copies ran while one was open for 1% of the time, Pallas kernels for 0%

profile of v1, /device:TPU:1, one launch (start us, length us, event | category | flops | bytes accessed | tf_op | source)
XLA Modules:
  0.0 234.9 jit_solution(6614310034171055877)
XLA Ops:
  0.6 1.8 copy.55
  2.4 0.0 copy-start.2
  2.4 8.7 %collective-permute-start.62 = (bf16[128,256]{0,1:T(8,128)(2,1)S(1)}, bf16[128,256]{0,1:T(8,128)(2,1)S(1)}, u32[]{:S(2)}, u32[]{:S(2)}) collective-permute-start(bf16[128,256]{0,1:T(8,128)(2,1)S(1)} %slice.76), channel_id=1, source_target_pairs={{1,0},{2,1},{3,2},{4,3},{5,4},{6,5},{7,6},{8,7},{9,8},{10,9},{11,1... | collective-permute-start | bytes 196616 | tf_op jit(solution)/shard_map/ppermute | solution.py:19
  11.2 1.3 multiply_convert_fusion.2
  12.5 0.3 copy.57
  12.8 0.1 convert_element_type.245
  13.0 1.4 pad_maximum_fusion.1
  14.4 0.6 fusion.21
  14.9 1.6 fusion
  16.6 1.9 copy.59
  18.5 1.4 reshape.384
  19.9 5.5 %all-to-all-start = ((bf16[128,2,2560]{2,1,0:T(2,128)(2,1)}), bf16[128,2,2560]{2,1,0:T(2,128)(2,1)S(1)}, u32[]{:S(2)}, u32[]{:S(2)}) async-start(bf16[128,2,2560]{2,1,0:T(2,128)(2,1)} %reshape.384), calls=%async_computation | async-start | bytes 2621440 | tf_op jit(solution)/shard_map/all_to_all | solution.py:70
  25.4 0.6 fusion.23
  27.3 18.0 %all-to-all-done = bf16[128,2,2560]{2,1,0:T(2,128)(2,1)S(1)} async-done(((bf16[128,2,2560]{2,1,0:T(2,128)(2,1)}), bf16[128,2,2560]{2,1,0:T(2,128)(2,1)S(1)}, u32[]{:S(2)}, u32[]{:S(2)}) %all-to-all-start) | async-done | bytes 1310752 | tf_op jit(solution)/shard_map/all_to_all | solution.py:70
  45.3 3.4 %multiply_reduce_fusion = f32[128,2560]{1,0:T(8,128)S(1)} fusion(bf16[128,2,2560]{2,1,0:T(2,128)(2,1)S(1)} %all-to-all-done), kind=kLoop, calls=%fused_computation.1 | loop fusion | flops 1638400 | bytes 2621440 | tf_op jit(solution)/shard_map/reduce_sum | solution.py:72
  48.8 1.8 copy.61
  50.6 1.4 reduce_sum.23
  52.0 0.1 reduce_sum.24
  52.0 0.9 convert_element_type.256
  53.0 3.0 %copy.60 = f32[8,2,16,2560]{3,2,1,0:T(8,128)} copy(f32[8,2,16,2560]{3,1,0,2:T(2,128)S(1)} %bitcast.84) | data formatting | bytes 5242880 | tf_op jit(solution)/shard_map/convert_element_type | solution.py:71
  55.9 2.5 %reshape.385 = f32[8,2,320,128]{3,2,1,0:T(8,128)S(1)} reshape(f32[8,2,16,2560]{3,2,1,0:T(8,128)} %copy.60) | data formatting | bytes 5242880 | tf_op jit(solution)/shard_map/convert_element_type | solution.py:71
  58.4 0.3 multiply_convert_fusion
  58.7 0.0 copy-start
  58.7 1.0 copy-done
  59.8 124.3 %conditional.2 = (bf16[8,2,320,128]{3,2,1,0:T(8,128)(2,1)}) conditional(s32[]{:T(128)} %bitcast, bf16[8,2,320,128]{3,2,1,0:T(8,128)(2,1)S(1)} %multiply_convert_fusion, bf16[8,2,320,128]{3,2,1,0:T(8,128)(2,1)S(1)} %multiply_convert_fusion, bf16[8,2,320,128]{3,2,1,0:T(8,128)(2,1)S(1)} %multiply_convert_fusion, ...), branch_computations={%region_2.3_spmd, %region_3.4_spmd, %region_4.5_spmd, %region_5.6_... | conditional | bytes 5242928 | solution.py:82
  59.8 11.1 %collective-permute-start.30 = (bf16[8,2,320,128]{3,2,1,0:T(8,128)(2,1)S(1)}, bf16[8,2,320,128]{3,2,1,0:T(8,128)(2,1)}, u32[]{:S(2)}, u32[]{:S(2)}) collective-permute-start(bf16[8,2,320,128]{3,2,1,0:T(8,128)(2,1)S(1)} %param.30), channel_id=1, source_target_pairs={{0,496},{16,480},{32,464},{48,448},{64,432},{80,416},{96,400},{112... | collective-permute-start | bytes 3932168 | tf_op jit(solution)/shard_map/cond/branch_30_fun/ppermute | solution.py:23
  70.9 113.1 %collective-permute-done.30 = bf16[8,2,320,128]{3,2,1,0:T(8,128)(2,1)} collective-permute-done((bf16[8,2,320,128]{3,2,1,0:T(8,128)(2,1)S(1)}, bf16[8,2,320,128]{3,2,1,0:T(8,128)(2,1)}, u32[]{:S(2)}, u32[]{:S(2)}) %collective-permute-start.30) | collective-permute-done | bytes 1310752 | tf_op jit(solution)/shard_map/cond/branch_30_fun/ppermute | solution.py:23
  184.1 2.5 %convolution_bitcast_fusion.2 = f32[8,2,2,128,128]{3,4,1,2,0:T(8,128)S(1)} fusion(bf16[8,2,320,128]{3,2,1,0:T(8,128)(2,1)} %get-tuple-element.146, bf16[8,2,320,128]{3,2,1,0:T(8,128)(2,1)} %copy-done), kind=kOutput, calls=%fused_computation.6 | convolution fusion | flops 335544320 | bytes 4718592 | tf_op jit(solution)/shard_map/kpwc,kqwd->kpqcd/dot_general | solution.py:38
  186.6 0.0 copy-start.1
  186.6 0.8 fusion.12
  187.4 0.8 fusion.14
  188.3 0.8 convolution_bitcast_fusion
  189.1 0.1 fusion.7
  189.2 0.9 fusion.9
  190.0 38.0 %conditional.3 = (bf16[8,2,320,128]{3,2,1,0:T(8,128)(2,1)}) conditional(s32[]{:T(128)} %bitcast.16, bf16[8,2,320,128]{3,2,1,0:T(8,128)(2,1)S(1)} %copy-done.1, bf16[8,2,320,128]{3,2,1,0:T(8,128)(2,1)S(1)} %copy-done.1, bf16[8,2,320,128]{3,2,1,0:T(8,128)(2,1)S(1)} %copy-done.1, ...), branch_computations={%region_33.34_spmd, %region_34.35_spmd, %region_35.36_spmd, %regio... | conditional | bytes 5242928 | solution.py:82
  190.0 7.2 %collective-permute-start.37 = (bf16[8,2,320,128]{3,2,1,0:T(8,128)(2,1)S(1)}, bf16[8,2,320,128]{3,2,1,0:T(8,128)(2,1)}, u32[]{:S(2)}, u32[]{:S(2)}) collective-permute-start(bf16[8,2,320,128]{3,2,1,0:T(8,128)(2,1)S(1)} %param.37), channel_id=1, source_target_pairs={{0,112},{16,96},{32,80},{48,64},{64,48},{80,32},{96,16},{112,0},{1... | collective-permute-start | bytes 3932168 | tf_op jit(solution)/shard_map/cond/branch_6_fun/ppermute | solution.py:23
  197.2 30.8 %collective-permute-done.37 = bf16[8,2,320,128]{3,2,1,0:T(8,128)(2,1)} collective-permute-done((bf16[8,2,320,128]{3,2,1,0:T(8,128)(2,1)S(1)}, bf16[8,2,320,128]{3,2,1,0:T(8,128)(2,1)}, u32[]{:S(2)}, u32[]{:S(2)}) %collective-permute-start.37) | collective-permute-done | bytes 1310752 | tf_op jit(solution)/shard_map/cond/branch_6_fun/ppermute | solution.py:23
  228.0 2.1 convolution_bitcast_fusion.1
  230.1 0.1 fusion.11
  230.2 0.0 copy-start.4
  230.3 0.1 maximum_multiply_fusion.1
  230.4 0.9 copy-done.4
  231.3 0.2 copy-done.5
  231.4 0.1 maximum_multiply_fusion
  231.5 0.1 pad_maximum_fusion
  231.7 1.8 copy.67
  233.5 0.1 maximum_multiply_fusion.2
  233.6 1.3 copy.68
  (14 shorter events, 0.1 us)
Async XLA Ops:
  0.6 10.6 %copy-start.7 = (s32[128]{0:T(128)S(1)}, s32[128]{0:T(128)}, u32[]{:S(2)}) copy-start(s32[128]{0:T(128)} %param.66) | copy-start | bytes 1540
  2.4 10.5 %copy-start.2 = (bf16[128,5120]{0,1:T(8,128)(2,1)}, bf16[128,5120]{0,1:T(8,128)(2,1)S(1)}, u32[]{:S(2)}) copy-start(bf16[128,5120]{0,1:T(8,128)(2,1)S(1)} %copy.55) | copy-start | bytes 3932164
  2.4 10.5 %collective-permute-start.62 = (bf16[128,256]{0,1:T(8,128)(2,1)S(1)}, bf16[128,256]{0,1:T(8,128)(2,1)S(1)}, u32[]{:S(2)}, u32[]{:S(2)}) collective-permute-start(bf16[128,256]{0,1:T(8,128)(2,1)S(1)} %slice.76), channel_id=1, source_target_pairs={{1,0},{2,1},{3,2},{4,3},{5,4},{6,5},{7,6},{8,7},{9,8},{10,9},{11,1... | collective-permute-start | bytes 196616 | tf_op jit(solution)/shard_map/ppermute | solution.py:19
  19.9 5.5 %copy-start.6 = (s32[2]{0:T(128)S(1)}, s32[2]{0:T(128)}, u32[]{:S(2)}) copy-start(s32[2]{0:T(128)} %param.67) | copy-start | bytes 28
  19.9 25.4 %all-to-all-start = ((bf16[128,2,2560]{2,1,0:T(2,128)(2,1)}), bf16[128,2,2560]{2,1,0:T(2,128)(2,1)S(1)}, u32[]{:S(2)}, u32[]{:S(2)}) async-start(bf16[128,2,2560]{2,1,0:T(2,128)(2,1)} %reshape.384), calls=%async_computation | async-start | bytes 2621440 | tf_op jit(solution)/shard_map/all_to_all | solution.py:70
  58.7 1.1 copy-start
  59.8 124.3 %collective-permute-start.30 = (bf16[8,2,320,128]{3,2,1,0:T(8,128)(2,1)S(1)}, bf16[8,2,320,128]{3,2,1,0:T(8,128)(2,1)}, u32[]{:S(2)}, u32[]{:S(2)}) collective-permute-start(bf16[8,2,320,128]{3,2,1,0:T(8,128)(2,1)S(1)} %param.30), channel_id=1, source_target_pairs={{0,496},{16,480},{32,464},{48,448},{64,432},{80,416},{96,400},{112... | collective-permute-start | bytes 3932168 | tf_op jit(solution)/shard_map/cond/branch_30_fun/ppermute | solution.py:23
  186.6 1.7 copy-start.1
  190.0 38.0 %collective-permute-start.37 = (bf16[8,2,320,128]{3,2,1,0:T(8,128)(2,1)S(1)}, bf16[8,2,320,128]{3,2,1,0:T(8,128)(2,1)}, u32[]{:S(2)}, u32[]{:S(2)}) collective-permute-start(bf16[8,2,320,128]{3,2,1,0:T(8,128)(2,1)S(1)} %param.37), channel_id=1, source_target_pairs={{0,112},{16,96},{32,80},{48,64},{64,48},{80,32},{96,16},{112,0},{1... | collective-permute-start | bytes 3932168 | tf_op jit(solution)/shard_map/cond/branch_6_fun/ppermute | solution.py:23
  230.2 1.0 copy-start.4
  230.2 1.2 copy-start.5
  231.7 1.8 copy-start.3
